TPU v7x, 512 devices: a whole 4x4x16 slice. The times are simulated.
512 devices in a mesh: gx: 64 (over z, y), gy: 8 (over x, core).
Axes of the slice: x: 4, y: 4, z: 16, core: 2. Of those that a mesh axis runs over, the one named last changes fastest.
Arguments:
- rhs: float32 [64, 8, 128, 128], P('gx', 'gy'), may hold values from -57 to 57
- face_rows: int32 [64, 8, 4, 128], P('gx', 'gy'), may hold values from 0 to 127
- margin_weight: float32 [64, 8, 4, 128], P('gx', 'gy'), may hold values from 0.2 to 1
- local_blocks: bfloat16 [64, 8, 1, 128, 128], P('gx', 'gy'), may hold values from -0.4 to 4.4
- subdomain_inverse: bfloat16 [64, 8, 128, 640], P('gx', 'gy'), may hold values from -0.4 to 1.8
- coarse_basis: bfloat16 [64, 8, 128, 32], P('gx', 'gy'), may hold values from -0.5 to 0.5
- coarse_inverse: bfloat16 [64, 8, 32, 16384], P('gx', 'gy'), may hold values from -0.09765625 to 0.09765625
- coarse_map: int32 [512], replicated, may hold values from 0 to 511, each once
Outputs:
- solution: float32 [64, 8, 128, 128], P('gx', 'gy')
- relative_residual: float32 [128], replicated
Inputs may be any that keep to these rules, and one draw needn't show every extreme that they name: `face_rows`: rows of the subdomain, repeats possible. `coarse_map`: every position once.
All inputs are finite; a program needn't handle non-finite values.
Results may differ from a plain program's by a relative error of at most 0.004.
Values may be sent and summed in bfloat16 or wider, within the bound.
No kernel may reach another device: no remote copies, remote signals or barrier semaphores. Data moves between devices by JAX's collectives and lax.ppermute only.
A program may use at most 64 MiB of HBM per device.

v0:
```python
import jax
import numpy as np
import jax.numpy as jnp
from jax import lax
from jax.sharding import PartitionSpec as P

EPSILON = 1e-06
KEPT_SHARE = 1.0 / 64


def neighbours(rows, axis):
    count = lax.axis_size(axis)
    up = [(i, i + 1) for i in range(count - 1)]
    down = [(i + 1, i) for i in range(count - 1)]
    return (lax.ppermute(rows[1], axis, up), lax.ppermute(rows[0], axis, down))


def exchange(packs):
    below_first, above_first = neighbours(packs[0:2], "gx")
    below_second, above_second = neighbours(packs[2:4], "gy")
    return jnp.stack([below_first, above_first, below_second, above_second], axis=0)


def allsum(value):
    value = lax.psum(value, "gy")
    for axis in ("gx",):
        count = lax.axis_size(axis)
        if count & count - 1:
            value = lax.psum(value, axis)
            continue
        step = 1
        while step < count:
            value = value + lax.ppermute(value, axis, [(i, i ^ step) for i in range(count)])
            step *= 2
    return value


GATHER_ROUNDS = (("gx", 32), ("gx", 16), ("gx", 8), ("gx", 4), ("gx", 2), ("gx", 1))


def gather_rounds(count_x, count_y):
    sizes = {"gx": count_x, "gy": count_y}
    return tuple(((axis, step) for axis, step in GATHER_ROUNDS if step < sizes[axis]))


def doubling_gather(block, rounds):
    held = block[None]
    for axis, step in rounds:
        count = lax.axis_size(axis)
        got = lax.ppermute(held, axis, [(i, i ^ step) for i in range(count)])
        upper = lax.axis_index(axis) // step % 2 == 1
        held = jnp.where(
            upper, jnp.concatenate([got, held], axis=0), jnp.concatenate([held, got], axis=0)
        )
    return lax.all_gather(held.reshape(-1, block.shape[-1]), "gy", axis=0, tiled=True)


def gathered_order(rounds, count_y):
    order = []
    for outer in range(count_y):
        for position in range(2 ** len(rounds)):
            index = {"gx": 0, "gy": outer}
            for bit, (axis, step) in enumerate(rounds):
                index[axis] += (position >> bit & 1) * step
            order.append(index["gx"] * count_y + index["gy"])
    return np.asarray(order, np.int32)


def least_squares(scale_norm, first_dot, first_norm, cross_dot, second_dot, second_norm):
    radius_one = jnp.sqrt(first_dot * first_dot + first_norm * first_norm)
    cosine_one = first_dot / radius_one
    sine_one = first_norm / radius_one
    upper_entry = cosine_one * cross_dot + sine_one * second_dot
    lower_entry = cosine_one * second_dot - sine_one * cross_dot
    radius_two = jnp.sqrt(lower_entry * lower_entry + second_norm * second_norm)
    cosine_two = lower_entry / radius_two
    sine_two = second_norm / radius_two
    weight_two = -cosine_two * sine_one * scale_norm / radius_two
    weight_one = (cosine_one * scale_norm - upper_entry * weight_two) / radius_one
    return (weight_one, weight_two, sine_one * sine_two)


def on_device(
    rhs,
    face_rows,
    margin_weight,
    local_blocks,
    subdomain_inverse,
    coarse_basis,
    coarse_inverse,
    coarse_map,
):
    right_side = rhs[0, 0]
    margin_rows = face_rows[0, 0]
    margin_weights = margin_weight[0, 0]
    local_block = local_blocks[0, 0]
    inverse_rows = subdomain_inverse[0, 0]
    basis = coarse_basis[0, 0]
    coarse_rows = coarse_inverse[0, 0]
    owned_rows = right_side.shape[0]
    system_count = right_side.shape[1]
    basis_count = basis.shape[1]
    block_rows = local_block.shape[1]
    count_x = lax.axis_size("gx")
    count_y = lax.axis_size("gy")
    rounds = gather_rounds(count_x, count_y)
    gathered_map = coarse_map[gathered_order(rounds, count_y)]
    selection = (
        gathered_map[:, None] == jnp.arange(gathered_map.shape[0], dtype=jnp.int32)[None, :]
    ).astype(jnp.bfloat16)

    def margin_of(field):
        return exchange(field[margin_rows])

    def coarse_gather(residual):
        return doubling_gather(residual, rounds)

    def precondition(rounded, margin):
        extended = jnp.concatenate([rounded, margin.reshape(-1, system_count)], axis=0)
        local_part = jnp.dot(inverse_rows, extended, preferred_element_type=jnp.float32)
        residual = lax.dot_general(
            basis, rounded, (((0,), (0,)), ((), ())), preferred_element_type=jnp.float32
        ).astype(jnp.bfloat16)
        gathered = coarse_gather(residual).reshape(selection.shape[0], -1)
        placed = lax.dot_general(
            selection, gathered, (((0,), (0,)), ((), ())), preferred_element_type=jnp.float32
        ).astype(jnp.bfloat16)
        solved = jnp.dot(
            coarse_rows, placed.reshape(-1, system_count), preferred_element_type=jnp.float32
        )
        return local_part + jnp.dot(
            basis, solved.astype(jnp.bfloat16), preferred_element_type=jnp.float32
        )

    def apply_operator(vector):
        rounded = vector.astype(jnp.bfloat16)
        own_part = jnp.einsum(
            "brc,bcn->brn",
            local_block,
            rounded.reshape(-1, block_rows, system_count),
            preferred_element_type=jnp.float32,
        ).reshape(owned_rows, system_count)
        weighted = margin_weights[:, :, None] * margin_of(rounded).astype(jnp.float32)
        coupling = (
            jnp.zeros((owned_rows, system_count), jnp.float32)
            .at[margin_rows.reshape(-1)]
            .add(weighted.reshape(-1, system_count))
        )
        return own_part - coupling

    def column_norm(vector):
        return jnp.sqrt(allsum(jnp.sum(vector * vector, axis=0)) + EPSILON)

    def guarded_norm(expanded, whole, remainder):
        kept = jnp.all(jnp.isfinite(expanded) & (expanded >= KEPT_SHARE * whole))
        return lax.cond(kept, lambda vector: jnp.sqrt(expanded + EPSILON), column_norm, remainder)

    rhs_margin = margin_of(right_side)
    scale_norm = column_norm(right_side)
    krylov_one = right_side / scale_norm
    margin_one = rhs_margin / scale_norm
    precond_one = precondition(krylov_one.astype(jnp.bfloat16), margin_one.astype(jnp.bfloat16))
    applied = apply_operator(precond_one)
    applied_margin = margin_of(applied)
    sums = allsum(
        jnp.stack(
            [
                jnp.sum(applied * krylov_one, axis=0),
                jnp.sum(applied * applied, axis=0),
                jnp.sum(krylov_one * krylov_one, axis=0),
            ]
        )
    )
    first_dot = sums[0]
    remainder = applied - first_dot * krylov_one
    expanded = sums[1] - 2.0 * first_dot * first_dot + first_dot * first_dot * sums[2]
    first_norm = guarded_norm(expanded, sums[1], remainder)
    krylov_two = remainder / first_norm
    margin_two = (applied_margin - first_dot * margin_one) / first_norm
    precond_two = precondition(krylov_two.astype(jnp.bfloat16), margin_two.astype(jnp.bfloat16))
    applied = apply_operator(precond_two)
    dots = allsum(
        jnp.stack(
            [
                jnp.sum(applied * krylov_one, axis=0),
                jnp.sum(applied * krylov_two, axis=0),
                jnp.sum(applied * applied, axis=0),
                jnp.sum(krylov_one * krylov_one, axis=0),
                jnp.sum(krylov_one * krylov_two, axis=0),
                jnp.sum(krylov_two * krylov_two, axis=0),
            ]
        )
    )
    cross_dot = dots[0]
    second_dot = dots[1]
    remainder = applied - cross_dot * krylov_one - second_dot * krylov_two
    expanded = (
        dots[2]
        - 2.0 * cross_dot * cross_dot
        - 2.0 * second_dot * second_dot
        + cross_dot * cross_dot * dots[3]
        + 2.0 * cross_dot * second_dot * dots[4]
        + second_dot * second_dot * dots[5]
    )
    second_norm = guarded_norm(expanded, dots[2], remainder)
    weight_one, weight_two, relative = least_squares(
        scale_norm, first_dot, first_norm, cross_dot, second_dot, second_norm
    )
    solution = weight_one * precond_one + weight_two * precond_two
    return (solution[None, None], relative)


def solution(mesh):
    return jax.shard_map(
        on_device,
        mesh=mesh,
        in_specs=(
            P("gx", "gy", None, None),
            P("gx", "gy", None, None),
            P("gx", "gy", None, None),
            P("gx", "gy", None, None, None),
            P("gx", "gy", None, None),
            P("gx", "gy", None, None),
            P("gx", "gy", None, None),
            P(),
        ),
        out_specs=(P("gx", "gy", None, None), P()),
        check_vma=False,
    )
```

profile of v0, /device:TPU:8, one launch (start us, length us, event | category | flops | bytes accessed | tf_op | source)
XLA Modules:
  0.0 481.7 jit_solution(6558370175424277475)
XLA Ops:
  8.2 14.6 %psum.35 = f32[128]{0:T(128)S(1)} all-reduce(f32[128]{0:T(128)S(1)} %multiply_reduce_fusion.10), channel_id=1, replica_groups=mesh['gx'=64,'gy'=8] {'gy'}, use_global_device_ids=true, to_apply=%region_1.0 | all-reduce | flops 128 | bytes 1024 | tf_op jit(solution)/shard_map/psum | solution.py:25
  22.8 5.5 %collective-permute-start.12 = (f32[128]{0:T(128)S(1)}, f32[128]{0:T(128)S(1)}, u32[]{:S(2)}, u32[]{:S(2)}) collective-permute-start(f32[128]{0:T(128)S(1)} %psum.35), channel_id=1, source_target_pairs={{0,8},{8,0},{16,24},{24,16},{32,40},{40,32},{48,56},{56,48},{64,72... | collective-permute-start | bytes 1544 | tf_op jit(solution)/shard_map/ppermute | solution.py:33
  32.5 4.3 collective-permute-done.13
  48.6 7.9 %collective-permute-start.16 = (f32[128]{0:T(128)S(1)}, f32[128]{0:T(128)S(1)}, u32[]{:S(2)}, u32[]{:S(2)}) collective-permute-start(f32[128]{0:T(128)S(1)} %add.222), channel_id=1, source_target_pairs={{0,128},{8,136},{16,144},{24,152},{32,160},{40,168},{48,176},{56,1... | collective-permute-start | bytes 1544 | tf_op jit(solution)/shard_map/ppermute | solution.py:33
  58.0 14.1 %collective-permute-start.17 = (f32[128]{0:T(128)S(1)}, f32[128]{0:T(128)S(1)}, u32[]{:S(2)}, u32[]{:S(2)}) collective-permute-start(f32[128]{0:T(128)S(1)} %add.223), channel_id=1, source_target_pairs={{0,256},{8,264},{16,272},{24,280},{32,288},{40,296},{48,304},{56,3... | collective-permute-start | bytes 1544 | tf_op jit(solution)/shard_map/ppermute | solution.py:33
  74.6 12.6 %collective-permute-start.22 = (bf16[1,32,128]{2,1,0:T(8,128)(2,1)S(1)}, bf16[1,32,128]{2,1,0:T(8,128)(2,1)S(1)}, u32[]{:S(2)}, u32[]{:S(2)}) collective-permute-start(bf16[1,32,128]{2,1,0:T(8,128)(2,1)S(1)} %fusion.2), channel_id=1, source_target_pairs={{0,256},{8,264},{16,272},{24,280},{32,288},{40,296},{48,304},{56,3... | collective-permute-start | bytes 24584 | tf_op jit(solution)/shard_map/ppermute | solution.py:50
  88.9 6.4 %collective-permute-start.23 = (bf16[2,32,128]{2,1,0:T(8,128)(2,1)S(1)}, bf16[2,32,128]{2,1,0:T(8,128)(2,1)S(1)}, u32[]{:S(2)}, u32[]{:S(2)}) collective-permute-start(bf16[2,32,128]{2,1,0:T(8,128)(2,1)S(1)} %maximum_select_fusion.10), channel_id=1, source_target_pairs={{0,128},{8,136},{16,144},{24,152},{32,160},{40,168},{48,176},{56,1... | collective-permute-start | bytes 49160 | tf_op jit(solution)/shard_map/ppermute | solution.py:50
  111.4 4.3 collective-permute-start.26
  115.7 4.1 collective-permute-done.26
  122.3 5.8 %collective-permute-done.27 = bf16[32,32,128]{2,1,0:T(8,128)(2,1)S(1)} collective-permute-done((bf16[32,32,128]{2,1,0:T(8,128)(2,1)S(1)}, bf16[32,32,128]{2,1,0:T(8,128)(2,1)S(1)}, u32[]{:S(2)}, u32[]{:S(2)}) %collective-permute-start.27) | collective-permute-done | bytes 262176 | tf_op jit(solution)/shard_map/ppermute | solution.py:50
  143.3 24.8 %all-gather.3.cloned.1.call-done = bf16[16384,128]{1,0:T(8,128)(2,1)} async-done(((bf16[2048,128]{1,0:T(8,128)(2,1)}), bf16[16384,128]{1,0:T(8,128)(2,1)}) %all-gather.3.cloned.1.call-update) | async-done | bytes 4194320 | tf_op jit(solution)/shard_map/all_gather | solution.py:55
  168.1 7.4 %reshape.132 = bf16[512,4096]{1,0:T(8,128)(2,1)} reshape(bf16[16384,128]{1,0:T(8,128)(2,1)} %all-gather.3.cloned.1.call-done) | data formatting | bytes 8388608 | tf_op jit(solution)/shard_map/reshape | solution.py:124
  175.4 6.6 %convolution_convert_fusion.1 = bf16[512,4096]{1,0:T(8,128)(2,1)} fusion(bf16[512,4096]{1,0:T(8,128)(2,1)} %reshape.132, s32[512]{0:T(512)S(1)} %gather_fusion.1), kind=kOutput, calls=%fused_computation.10 | convolution fusion | flops 2149842944 | bytes 8390656 | tf_op jit(solution)/shard_map/dot_general | solution.py:125
  182.0 7.5 %reshape.133 = bf16[16384,128]{1,0:T(8,128)(2,1)} reshape(bf16[512,4096]{1,0:T(8,128)(2,1)} %convolution_convert_fusion.1) | data formatting | bytes 8388608 | tf_op jit(solution)/shard_map/reshape | solution.py:129
  208.4 14.6 %psum.36 = f32[3,128]{1,0:T(4,128)S(1)} all-reduce(f32[3,128]{1,0:T(4,128)S(1)} %pad_maximum_fusion.4), channel_id=1, replica_groups=mesh['gx'=64,'gy'=8] {'gy'}, use_global_device_ids=true, to_apply=%region_6.7 | all-reduce | flops 384 | bytes 3072 | tf_op jit(solution)/shard_map/psum | solution.py:25
  235.4 4.1 collective-permute-start.34
  241.1 4.9 %collective-permute-start.35 = (f32[3,128]{1,0:T(4,128)S(1)}, f32[3,128]{1,0:T(4,128)S(1)}, u32[]{:S(2)}, u32[]{:S(2)}) collective-permute-start(f32[3,128]{1,0:T(4,128)S(1)} %add.239), channel_id=1, source_target_pairs={{0,64},{8,72},{16,80},{24,88},{32,96},{40,104},{48,112},{56,120},{... | collective-permute-start | bytes 4616 | tf_op jit(solution)/shard_map/ppermute | solution.py:33
  247.6 9.2 %collective-permute-start.36 = (f32[3,128]{1,0:T(4,128)S(1)}, f32[3,128]{1,0:T(4,128)S(1)}, u32[]{:S(2)}, u32[]{:S(2)}) collective-permute-start(f32[3,128]{1,0:T(4,128)S(1)} %add.240), channel_id=1, source_target_pairs={{0,128},{8,136},{16,144},{24,152},{32,160},{40,168},{48,176},{56,1... | collective-permute-start | bytes 4616 | tf_op jit(solution)/shard_map/ppermute | solution.py:33
  258.3 13.0 %collective-permute-start.37 = (f32[3,128]{1,0:T(4,128)S(1)}, f32[3,128]{1,0:T(4,128)S(1)}, u32[]{:S(2)}, u32[]{:S(2)}) collective-permute-start(f32[3,128]{1,0:T(4,128)S(1)} %add.241), channel_id=1, source_target_pairs={{0,256},{8,264},{16,272},{24,280},{32,288},{40,296},{48,304},{56,3... | collective-permute-start | bytes 4616 | tf_op jit(solution)/shard_map/ppermute | solution.py:33
  274.4 12.6 %collective-permute-start.42 = (bf16[1,32,128]{2,1,0:T(8,128)(2,1)S(1)}, bf16[1,32,128]{2,1,0:T(8,128)(2,1)S(1)}, u32[]{:S(2)}, u32[]{:S(2)}) collective-permute-start(bf16[1,32,128]{2,1,0:T(8,128)(2,1)S(1)} %fusion.3), channel_id=1, source_target_pairs={{0,256},{8,264},{16,272},{24,280},{32,288},{40,296},{48,304},{56,3... | collective-permute-start | bytes 24584 | tf_op jit(solution)/shard_map/ppermute | solution.py:50
  288.6 7.5 %collective-permute-start.43 = (bf16[2,32,128]{2,1,0:T(8,128)(2,1)S(1)}, bf16[2,32,128]{2,1,0:T(8,128)(2,1)S(1)}, u32[]{:S(2)}, u32[]{:S(2)}) collective-permute-start(bf16[2,32,128]{2,1,0:T(8,128)(2,1)S(1)} %maximum_select_fusion.11), channel_id=1, source_target_pairs={{0,128},{8,136},{16,144},{24,152},{32,160},{40,168},{48,176},{56,1... | collective-permute-start | bytes 49160 | tf_op jit(solution)/shard_map/ppermute | solution.py:50
  314.7 4.7 collective-permute-done.46
  323.4 4.3 collective-permute-done.47
  340.4 26.8 %all-gather.5.cloned.1.call-done = bf16[16384,128]{1,0:T(8,128)(2,1)} async-done(((bf16[2048,128]{1,0:T(8,128)(2,1)}), bf16[16384,128]{1,0:T(8,128)(2,1)}) %all-gather.5.cloned.1.call-update) | async-done | bytes 4194320 | tf_op jit(solution)/shard_map/all_gather | solution.py:55
  367.2 7.4 %reshape.135 = bf16[512,4096]{1,0:T(8,128)(2,1)} reshape(bf16[16384,128]{1,0:T(8,128)(2,1)} %all-gather.5.cloned.1.call-done) | data formatting | bytes 8388608 | tf_op jit(solution)/shard_map/reshape | solution.py:124
  374.6 6.6 %convolution_convert_fusion = bf16[512,4096]{1,0:T(8,128)(2,1)} fusion(bf16[512,4096]{1,0:T(8,128)(2,1)} %reshape.135, s32[512]{0:T(512)S(1)} %gather_fusion.1), kind=kOutput, calls=%fused_computation.9 | convolution fusion | flops 2149842944 | bytes 8390656 | tf_op jit(solution)/shard_map/dot_general | solution.py:125
  381.2 7.4 %reshape.136 = bf16[16384,128]{1,0:T(8,128)(2,1)} reshape(bf16[512,4096]{1,0:T(8,128)(2,1)} %convolution_convert_fusion) | data formatting | bytes 8388608 | tf_op jit(solution)/shard_map/reshape | solution.py:129
  407.4 14.6 %psum.37 = f32[6,128]{1,0:T(8,128)S(1)} all-reduce(f32[6,128]{1,0:T(8,128)S(1)} %stack.126), channel_id=1, replica_groups=mesh['gx'=64,'gy'=8] {'gy'}, use_global_device_ids=true, to_apply=%region_18.19 | all-reduce | flops 768 | bytes 6144 | tf_op jit(solution)/shard_map/psum | solution.py:25
  434.6 4.1 collective-permute-start.54
  440.2 4.9 %collective-permute-start.55 = (f32[6,128]{1,0:T(8,128)S(1)}, f32[6,128]{1,0:T(8,128)S(1)}, u32[]{:S(2)}, u32[]{:S(2)}) collective-permute-start(f32[6,128]{1,0:T(8,128)S(1)} %add.249), channel_id=1, source_target_pairs={{0,64},{8,72},{16,80},{24,88},{32,96},{40,104},{48,112},{56,120},{... | collective-permute-start | bytes 9224 | tf_op jit(solution)/shard_map/ppermute | solution.py:33
  446.7 9.2 %collective-permute-start.56 = (f32[6,128]{1,0:T(8,128)S(1)}, f32[6,128]{1,0:T(8,128)S(1)}, u32[]{:S(2)}, u32[]{:S(2)}) collective-permute-start(f32[6,128]{1,0:T(8,128)S(1)} %add.250), channel_id=1, source_target_pairs={{0,128},{8,136},{16,144},{24,152},{32,160},{40,168},{48,176},{56,1... | collective-permute-start | bytes 9224 | tf_op jit(solution)/shard_map/ppermute | solution.py:33
  457.5 13.0 %collective-permute-start.57 = (f32[6,128]{1,0:T(8,128)S(1)}, f32[6,128]{1,0:T(8,128)S(1)}, u32[]{:S(2)}, u32[]{:S(2)}) collective-permute-start(f32[6,128]{1,0:T(8,128)S(1)} %add.251), channel_id=1, source_target_pairs={{0,256},{8,264},{16,272},{24,280},{32,288},{40,296},{48,304},{56,3... | collective-permute-start | bytes 9224 | tf_op jit(solution)/shard_map/ppermute | solution.py:33
  (173 shorter events, 170.4 us)
Async XLA Ops:
  7.2 160.9 %all-gather.3.cloned.1.call-start = ((), (), s32[]{:S(2)}) async-start(), calls=%async_computation | async-start | bytes 4718592 | tf_op jit(solution)/shard_map/all_gather | solution.py:55
  22.8 7.0 %collective-permute-start.12 = (f32[128]{0:T(128)S(1)}, f32[128]{0:T(128)S(1)}, u32[]{:S(2)}, u32[]{:S(2)}) collective-permute-start(f32[128]{0:T(128)S(1)} %psum.35), channel_id=1, source_target_pairs={{0,8},{8,0},{16,24},{24,16},{32,40},{40,32},{48,56},{56,48},{64,72... | collective-permute-start | bytes 1544 | tf_op jit(solution)/shard_map/ppermute | solution.py:33
  29.9 7.0 %collective-permute-start.13 = (f32[128]{0:T(128)S(1)}, f32[128]{0:T(128)S(1)}, u32[]{:S(2)}, u32[]{:S(2)}) collective-permute-start(f32[128]{0:T(128)S(1)} %add.219), channel_id=1, source_target_pairs={{0,16},{8,24},{16,0},{24,8},{32,48},{40,56},{48,32},{56,40},{64,80... | collective-permute-start | bytes 1544 | tf_op jit(solution)/shard_map/ppermute | solution.py:33
  42.3 6.3 %collective-permute-start.15 = (f32[128]{0:T(128)S(1)}, f32[128]{0:T(128)S(1)}, u32[]{:S(2)}, u32[]{:S(2)}) collective-permute-start(f32[128]{0:T(128)S(1)} %add.221), channel_id=1, source_target_pairs={{0,64},{8,72},{16,80},{24,88},{32,96},{40,104},{48,112},{56,120},{... | collective-permute-start | bytes 1544 | tf_op jit(solution)/shard_map/ppermute | solution.py:33
  48.6 9.4 %collective-permute-start.16 = (f32[128]{0:T(128)S(1)}, f32[128]{0:T(128)S(1)}, u32[]{:S(2)}, u32[]{:S(2)}) collective-permute-start(f32[128]{0:T(128)S(1)} %add.222), channel_id=1, source_target_pairs={{0,128},{8,136},{16,144},{24,152},{32,160},{40,168},{48,176},{56,1... | collective-permute-start | bytes 1544 | tf_op jit(solution)/shard_map/ppermute | solution.py:33
  58.0 15.6 %collective-permute-start.17 = (f32[128]{0:T(128)S(1)}, f32[128]{0:T(128)S(1)}, u32[]{:S(2)}, u32[]{:S(2)}) collective-permute-start(f32[128]{0:T(128)S(1)} %add.223), channel_id=1, source_target_pairs={{0,256},{8,264},{16,272},{24,280},{32,288},{40,296},{48,304},{56,3... | collective-permute-start | bytes 1544 | tf_op jit(solution)/shard_map/ppermute | solution.py:33
  74.6 14.3 %collective-permute-start.22 = (bf16[1,32,128]{2,1,0:T(8,128)(2,1)S(1)}, bf16[1,32,128]{2,1,0:T(8,128)(2,1)S(1)}, u32[]{:S(2)}, u32[]{:S(2)}) collective-permute-start(bf16[1,32,128]{2,1,0:T(8,128)(2,1)S(1)} %fusion.2), channel_id=1, source_target_pairs={{0,256},{8,264},{16,272},{24,280},{32,288},{40,296},{48,304},{56,3... | collective-permute-start | bytes 24584 | tf_op jit(solution)/shard_map/ppermute | solution.py:50
  88.9 9.5 %collective-permute-start.23 = (bf16[2,32,128]{2,1,0:T(8,128)(2,1)S(1)}, bf16[2,32,128]{2,1,0:T(8,128)(2,1)S(1)}, u32[]{:S(2)}, u32[]{:S(2)}) collective-permute-start(bf16[2,32,128]{2,1,0:T(8,128)(2,1)S(1)} %maximum_select_fusion.10), channel_id=1, source_target_pairs={{0,128},{8,136},{16,144},{24,152},{32,160},{40,168},{48,176},{56,1... | collective-permute-start | bytes 49160 | tf_op jit(solution)/shard_map/ppermute | solution.py:50
  98.5 6.7 %collective-permute-start.24 = (bf16[4,32,128]{2,1,0:T(8,128)(2,1)S(1)}, bf16[4,32,128]{2,1,0:T(8,128)(2,1)S(1)}, u32[]{:S(2)}, u32[]{:S(2)}) collective-permute-start(bf16[4,32,128]{2,1,0:T(8,128)(2,1)S(1)} %maximum_select_fusion.8), channel_id=1, source_target_pairs={{0,64},{8,72},{16,80},{24,88},{32,96},{40,104},{48,112},{56,120},{... | collective-permute-start | bytes 98312 | tf_op jit(solution)/shard_map/ppermute | solution.py:50
  111.4 8.5 %collective-permute-start.26 = (bf16[16,32,128]{2,1,0:T(8,128)(2,1)S(1)}, bf16[16,32,128]{2,1,0:T(8,128)(2,1)S(1)}, u32[]{:S(2)}, u32[]{:S(2)}) collective-permute-start(bf16[16,32,128]{2,1,0:T(8,128)(2,1)S(1)} %maximum_select_fusion.4), channel_id=1, source_target_pairs={{0,16},{8,24},{16,0},{24,8},{32,48},{40,56},{48,32},{56,40},{64,80... | collective-permute-start | bytes 393224 | tf_op jit(solution)/shard_map/ppermute | solution.py:50
  119.9 8.3 %collective-permute-start.27 = (bf16[32,32,128]{2,1,0:T(8,128)(2,1)S(1)}, bf16[32,32,128]{2,1,0:T(8,128)(2,1)S(1)}, u32[]{:S(2)}, u32[]{:S(2)}) collective-permute-start(bf16[32,32,128]{2,1,0:T(8,128)(2,1)S(1)} %maximum_select_fusion.2), channel_id=1, source_target_pairs={{0,8},{8,0},{16,24},{24,16},{32,40},{40,32},{48,56},{56,48},{64,72... | collective-permute-start | bytes 786440 | tf_op jit(solution)/shard_map/ppermute | solution.py:50
  129.1 238.1 %all-gather.5.cloned.1.call-start = ((), (), s32[]{:S(2)}) async-start(), calls=%async_computation.1 | async-start | bytes 4718592 | tf_op jit(solution)/shard_map/all_gather | solution.py:55
  130.9 12.0 %collective-permute-start.18 = (f32[128,128]{1,0:T(8,128)S(1)}, f32[128,128]{1,0:T(8,128)S(1)}, u32[]{:S(2)}, u32[]{:S(2)}) collective-permute-start(f32[128,128]{1,0:T(8,128)S(1)} %get-tuple-element.64), channel_id=1, source_target_pairs={{0,8},{8,16},{16,24},{24,32},{32,40},{40,48},{48,56},{56,64},{64,7... | collective-permute-start | bytes 196616 | tf_op jit(solution)/shard_map/ppermute | solution.py:15
  134.4 8.5 %collective-permute-start.20 = (f32[128,128]{1,0:T(8,128)S(1)}, f32[128,128]{1,0:T(8,128)S(1)}, u32[]{:S(2)}, u32[]{:S(2)}) collective-permute-start(f32[128,128]{1,0:T(8,128)S(1)} %get-tuple-element.65), channel_id=1, source_target_pairs={{0,1},{1,2},{2,3},{3,4},{4,5},{5,6},{6,7},{8,9},{9,10},{10,11},{11... | collective-permute-start | bytes 196616 | tf_op jit(solution)/shard_map/ppermute | solution.py:15
  135.7 7.2 %collective-permute-start.19 = (f32[128,128]{1,0:T(8,128)S(1)}, f32[128,128]{1,0:T(8,128)S(1)}, u32[]{:S(2)}, u32[]{:S(2)}) collective-permute-start(f32[128,128]{1,0:T(8,128)S(1)} %get-tuple-element.66), channel_id=1, source_target_pairs={{8,0},{16,8},{24,16},{32,24},{40,32},{48,40},{56,48},{64,56},{72,6... | collective-permute-start | bytes 196616 | tf_op jit(solution)/shard_map/ppermute | solution.py:15
  194.6 9.1 %collective-permute-start.28 = (bf16[128,128]{1,0:T(8,128)(2,1)S(1)}, bf16[128,128]{1,0:T(8,128)(2,1)S(1)}, u32[]{:S(2)}, u32[]{:S(2)}) collective-permute-start(bf16[128,128]{1,0:T(8,128)(2,1)S(1)} %get-tuple-element.72), channel_id=1, source_target_pairs={{0,8},{8,16},{16,24},{24,32},{32,40},{40,48},{48,56},{56,64},{64,7... | collective-permute-start | bytes 98312 | tf_op jit(solution)/shard_map/ppermute | solution.py:15
  228.5 7.0 %collective-permute-start.33 = (f32[3,128]{1,0:T(4,128)S(1)}, f32[3,128]{1,0:T(4,128)S(1)}, u32[]{:S(2)}, u32[]{:S(2)}) collective-permute-start(f32[3,128]{1,0:T(4,128)S(1)} %add.237), channel_id=1, source_target_pairs={{0,16},{8,24},{16,0},{24,8},{32,48},{40,56},{48,32},{56,40},{64,80... | collective-permute-start | bytes 4616 | tf_op jit(solution)/shard_map/ppermute | solution.py:33
  241.1 6.5 %collective-permute-start.35 = (f32[3,128]{1,0:T(4,128)S(1)}, f32[3,128]{1,0:T(4,128)S(1)}, u32[]{:S(2)}, u32[]{:S(2)}) collective-permute-start(f32[3,128]{1,0:T(4,128)S(1)} %add.239), channel_id=1, source_target_pairs={{0,64},{8,72},{16,80},{24,88},{32,96},{40,104},{48,112},{56,120},{... | collective-permute-start | bytes 4616 | tf_op jit(solution)/shard_map/ppermute | solution.py:33
  247.6 10.8 %collective-permute-start.36 = (f32[3,128]{1,0:T(4,128)S(1)}, f32[3,128]{1,0:T(4,128)S(1)}, u32[]{:S(2)}, u32[]{:S(2)}) collective-permute-start(f32[3,128]{1,0:T(4,128)S(1)} %add.240), channel_id=1, source_target_pairs={{0,128},{8,136},{16,144},{24,152},{32,160},{40,168},{48,176},{56,1... | collective-permute-start | bytes 4616 | tf_op jit(solution)/shard_map/ppermute | solution.py:33
  258.3 14.5 %collective-permute-start.37 = (f32[3,128]{1,0:T(4,128)S(1)}, f32[3,128]{1,0:T(4,128)S(1)}, u32[]{:S(2)}, u32[]{:S(2)}) collective-permute-start(f32[3,128]{1,0:T(4,128)S(1)} %add.241), channel_id=1, source_target_pairs={{0,256},{8,264},{16,272},{24,280},{32,288},{40,296},{48,304},{56,3... | collective-permute-start | bytes 4616 | tf_op jit(solution)/shard_map/ppermute | solution.py:33
  274.4 14.3 %collective-permute-start.42 = (bf16[1,32,128]{2,1,0:T(8,128)(2,1)S(1)}, bf16[1,32,128]{2,1,0:T(8,128)(2,1)S(1)}, u32[]{:S(2)}, u32[]{:S(2)}) collective-permute-start(bf16[1,32,128]{2,1,0:T(8,128)(2,1)S(1)} %fusion.3), channel_id=1, source_target_pairs={{0,256},{8,264},{16,272},{24,280},{32,288},{40,296},{48,304},{56,3... | collective-permute-start | bytes 24584 | tf_op jit(solution)/shard_map/ppermute | solution.py:50
  288.6 9.5 %collective-permute-start.43 = (bf16[2,32,128]{2,1,0:T(8,128)(2,1)S(1)}, bf16[2,32,128]{2,1,0:T(8,128)(2,1)S(1)}, u32[]{:S(2)}, u32[]{:S(2)}) collective-permute-start(bf16[2,32,128]{2,1,0:T(8,128)(2,1)S(1)} %maximum_select_fusion.11), channel_id=1, source_target_pairs={{0,128},{8,136},{16,144},{24,152},{32,160},{40,168},{48,176},{56,1... | collective-permute-start | bytes 49160 | tf_op jit(solution)/shard_map/ppermute | solution.py:50
  298.2 6.7 %collective-permute-start.44 = (bf16[4,32,128]{2,1,0:T(8,128)(2,1)S(1)}, bf16[4,32,128]{2,1,0:T(8,128)(2,1)S(1)}, u32[]{:S(2)}, u32[]{:S(2)}) collective-permute-start(bf16[4,32,128]{2,1,0:T(8,128)(2,1)S(1)} %maximum_select_fusion.9), channel_id=1, source_target_pairs={{0,64},{8,72},{16,80},{24,88},{32,96},{40,104},{48,112},{56,120},{... | collective-permute-start | bytes 98312 | tf_op jit(solution)/shard_map/ppermute | solution.py:50
  311.1 8.4 %collective-permute-start.46 = (bf16[16,32,128]{2,1,0:T(8,128)(2,1)S(1)}, bf16[16,32,128]{2,1,0:T(8,128)(2,1)S(1)}, u32[]{:S(2)}, u32[]{:S(2)}) collective-permute-start(bf16[16,32,128]{2,1,0:T(8,128)(2,1)S(1)} %maximum_select_fusion.5), channel_id=1, source_target_pairs={{0,16},{8,24},{16,0},{24,8},{32,48},{40,56},{48,32},{56,40},{64,80... | collective-permute-start | bytes 393224 | tf_op jit(solution)/shard_map/ppermute | solution.py:50
  319.5 8.3 %collective-permute-start.47 = (bf16[32,32,128]{2,1,0:T(8,128)(2,1)S(1)}, bf16[32,32,128]{2,1,0:T(8,128)(2,1)S(1)}, u32[]{:S(2)}, u32[]{:S(2)}) collective-permute-start(bf16[32,32,128]{2,1,0:T(8,128)(2,1)S(1)} %maximum_select_fusion.3), channel_id=1, source_target_pairs={{0,8},{8,0},{16,24},{24,16},{32,40},{40,32},{48,56},{56,48},{64,72... | collective-permute-start | bytes 786440 | tf_op jit(solution)/shard_map/ppermute | solution.py:50
  329.7 8.6 %collective-permute-start.38 = (f32[128,128]{1,0:T(8,128)S(1)}, f32[128,128]{1,0:T(8,128)S(1)}, u32[]{:S(2)}, u32[]{:S(2)}) collective-permute-start(f32[128,128]{1,0:T(8,128)S(1)} %get-tuple-element.60), channel_id=1, source_target_pairs={{0,8},{8,16},{16,24},{24,32},{32,40},{40,48},{48,56},{56,64},{64,7... | collective-permute-start | bytes 196616 | tf_op jit(solution)/shard_map/ppermute | solution.py:15
  331.9 6.5 %collective-permute-start.40 = (f32[128,128]{1,0:T(8,128)S(1)}, f32[128,128]{1,0:T(8,128)S(1)}, u32[]{:S(2)}, u32[]{:S(2)}) collective-permute-start(f32[128,128]{1,0:T(8,128)S(1)} %get-tuple-element.61), channel_id=1, source_target_pairs={{0,1},{1,2},{2,3},{3,4},{4,5},{5,6},{6,7},{8,9},{9,10},{10,11},{11... | collective-permute-start | bytes 196616 | tf_op jit(solution)/shard_map/ppermute | solution.py:15
  393.7 9.0 %collective-permute-start.48 = (bf16[128,128]{1,0:T(8,128)(2,1)S(1)}, bf16[128,128]{1,0:T(8,128)(2,1)S(1)}, u32[]{:S(2)}, u32[]{:S(2)}) collective-permute-start(bf16[128,128]{1,0:T(8,128)(2,1)S(1)} %get-tuple-element.68), channel_id=1, source_target_pairs={{0,8},{8,16},{16,24},{24,32},{32,40},{40,48},{48,56},{56,64},{64,7... | collective-permute-start | bytes 98312 | tf_op jit(solution)/shard_map/ppermute | solution.py:15
  427.6 7.0 %collective-permute-start.53 = (f32[6,128]{1,0:T(8,128)S(1)}, f32[6,128]{1,0:T(8,128)S(1)}, u32[]{:S(2)}, u32[]{:S(2)}) collective-permute-start(f32[6,128]{1,0:T(8,128)S(1)} %add.247), channel_id=1, source_target_pairs={{0,16},{8,24},{16,0},{24,8},{32,48},{40,56},{48,32},{56,40},{64,80... | collective-permute-start | bytes 9224 | tf_op jit(solution)/shard_map/ppermute | solution.py:33
  440.2 6.5 %collective-permute-start.55 = (f32[6,128]{1,0:T(8,128)S(1)}, f32[6,128]{1,0:T(8,128)S(1)}, u32[]{:S(2)}, u32[]{:S(2)}) collective-permute-start(f32[6,128]{1,0:T(8,128)S(1)} %add.249), channel_id=1, source_target_pairs={{0,64},{8,72},{16,80},{24,88},{32,96},{40,104},{48,112},{56,120},{... | collective-permute-start | bytes 9224 | tf_op jit(solution)/shard_map/ppermute | solution.py:33
  446.7 10.8 %collective-permute-start.56 = (f32[6,128]{1,0:T(8,128)S(1)}, f32[6,128]{1,0:T(8,128)S(1)}, u32[]{:S(2)}, u32[]{:S(2)}) collective-permute-start(f32[6,128]{1,0:T(8,128)S(1)} %add.250), channel_id=1, source_target_pairs={{0,128},{8,136},{16,144},{24,152},{32,160},{40,168},{48,176},{56,1... | collective-permute-start | bytes 9224 | tf_op jit(solution)/shard_map/ppermute | solution.py:33
  457.5 14.6 %collective-permute-start.57 = (f32[6,128]{1,0:T(8,128)S(1)}, f32[6,128]{1,0:T(8,128)S(1)}, u32[]{:S(2)}, u32[]{:S(2)}) collective-permute-start(f32[6,128]{1,0:T(8,128)S(1)} %add.251), channel_id=1, source_target_pairs={{0,256},{8,264},{16,272},{24,280},{32,288},{40,296},{48,304},{56,3... | collective-permute-start | bytes 9224 | tf_op jit(solution)/shard_map/ppermute | solution.py:33
  (25 other events, 741.4 us)
Sparse Core Ops, SparseCore 0:
  129.2 38.8 all-gather.2
  328.8 38.3 all-gather.4
where the time goes:
time: 484 us; the launch traced here: 482 us
  starting transfers between devices  210 us (43%)
  waiting for transfers between devices  139 us (29%)
  blocking collectives  43.9 us (9%)
  local copies, waits for them, and re-layouts  39 us (8%)
  matrix products  22.4 us (5%)
  between operations  16.4 us (3%)
  other arithmetic  10.6 us (2%)
    ppermute x18, starting transfers between devices, allsum(): lax.ppermute(value, axis, [(i, i ^ step) for i in range(count)])  110 us
    ppermute x12, starting transfers between devices, doubling_gather(): got = lax.ppermute(held, axis, [(i, i ^ step) for i in range(count)])  65.1 us
    all_gather x2, waiting for transfers between devices, doubling_gather(): lax.all_gather(held.reshape(-1, block.shape[-1]), 'gy', axis=0, tiled=True)  51.6 us
    psum x3, blocking collectives, allsum(): value = lax.psum(value, 'gy')  43.9 us
    ppermute x12, waiting for transfers between devices, doubling_gather(): got = lax.ppermute(held, axis, [(i, i ^ step) for i in range(count)])  41.3 us
    ppermute x18, waiting for transfers between devices, allsum(): lax.ppermute(value, axis, [(i, i ^ step) for i in range(count)])  40.5 us
    ppermute x16, starting transfers between devices, neighbours(): return (lax.ppermute(rows[1], axis, up), lax.ppermute(rows[0], axis, down))  35 us
    reshape x2, local copies, waits for them, and re-layouts, precondition(): placed.reshape(-1, system_count)  14.9 us
  transfers between devices with their start and end apart: 48, of which 36 were waited for; matrix products, arithmetic and copies ran while one was open for 1% of the time, Pallas kernels for 0%

commit v1 on v0

--- a/solution.py
+++ b/solution.py
@@ -52,7 +52,12 @@
         held = jnp.where(
             upper, jnp.concatenate([got, held], axis=0), jnp.concatenate([held, got], axis=0)
         )
-    return lax.all_gather(held.reshape(-1, block.shape[-1]), "gy", axis=0, tiled=True)
+    return jnp.concatenate(
+        lax.all_to_all(
+            jnp.stack([held.reshape(-1, block.shape[-1])] * lax.axis_size("gy")), "gy", 0, 0
+        ),
+        axis=0,
+    )
 
 
 def gathered_order(rounds, count_y):

time: 484 us -> 508 us (1.050)
  the two profiles are of different devices: /device:TPU:8 before, /device:TPU:384 now
where the time goes in v1:
time: 508 us; the launch traced here: 506 us
  waiting for transfers between devices  243 us (48%)
  starting transfers between devices  145 us (29%)
  local copies, waits for them, and re-layouts  44 us (9%)
  blocking collectives  39.4 us (8%)
  matrix products  22.3 us (4%)
  other arithmetic  8.34 us (2%)
    ppermute x18, waiting for transfers between devices, allsum(): lax.ppermute(value, axis, [(i, i ^ step) for i in range(count)])  91.6 us
    ppermute x12, waiting for transfers between devices, doubling_gather(): got = lax.ppermute(held, axis, [(i, i ^ step) for i in range(count)])  68.5 us
    all_to_all x2, waiting for transfers between devices, doubling_gather(): lax.all_to_all(jnp.stack([held.reshape(-1, block.shape[-1])] * lax.axis_s...  61 us
    ppermute x18, starting transfers between devices, allsum(): lax.ppermute(value, axis, [(i, i ^ step) for i in range(count)])  51.8 us
    ppermute x16, starting transfers between devices, neighbours(): return (lax.ppermute(rows[1], axis, up), lax.ppermute(rows[0], axis, down))  46 us
    psum x3, blocking collectives, allsum(): value = lax.psum(value, 'gy')  39.4 us
    ppermute x12, starting transfers between devices, doubling_gather(): got = lax.ppermute(held, axis, [(i, i ^ step) for i in range(count)])  38.3 us
    ppermute x16, waiting for transfers between devices, neighbours(): return (lax.ppermute(rows[1], axis, up), lax.ppermute(rows[0], axis, down))  22.3 us
  transfers between devices with their start and end apart: 48, of which 37 were waited for; matrix products, arithmetic and copies ran while one was open for 1% of the time, Pallas kernels for 0%

profile of v1, /device:TPU:384, one launch (start us, length us, event | category | flops | bytes accessed | tf_op | source)
XLA Modules:
  0.0 505.8 jit_solution(14532662825605448992)
XLA Ops:
  1.6 14.6 %psum.35 = f32[128]{0:T(128)S(1)} all-reduce(f32[128]{0:T(128)S(1)} %multiply_reduce_fusion.10), channel_id=1, replica_groups=mesh['gx'=64,'gy'=8] {'gy'}, use_global_device_ids=true, to_apply=%region_1.0 | all-reduce | flops 128 | bytes 1024 | tf_op jit(solution)/shard_map/psum | solution.py:25
  21.7 5.1 %collective-permute-start.13 = (f32[128]{0:T(128)S(1)}, f32[128]{0:T(128)S(1)}, u32[]{:S(2)}, u32[]{:S(2)}) collective-permute-start(f32[128]{0:T(128)S(1)} %add.219), channel_id=1, source_target_pairs={{0,16},{8,24},{16,0},{24,8},{32,48},{40,56},{48,32},{56,40},{64,80... | collective-permute-start | bytes 1544 | tf_op jit(solution)/shard_map/ppermute | solution.py:33
  40.4 5.4 %collective-permute-start.16 = (f32[128]{0:T(128)S(1)}, f32[128]{0:T(128)S(1)}, u32[]{:S(2)}, u32[]{:S(2)}) collective-permute-start(f32[128]{0:T(128)S(1)} %add.222), channel_id=1, source_target_pairs={{0,128},{8,136},{16,144},{24,152},{32,160},{40,168},{48,176},{56,1... | collective-permute-start | bytes 1544 | tf_op jit(solution)/shard_map/ppermute | solution.py:33
  53.8 10.2 %collective-permute-done.17 = f32[128]{0:T(128)S(1)} collective-permute-done((f32[128]{0:T(128)S(1)}, f32[128]{0:T(128)S(1)}, u32[]{:S(2)}, u32[]{:S(2)}) %collective-permute-start.17) | collective-permute-done | bytes 544 | tf_op jit(solution)/shard_map/ppermute | solution.py:33
  69.0 10.2 %collective-permute-done.22 = bf16[1,32,128]{2,1,0:T(8,128)(2,1)S(1)} collective-permute-done((bf16[1,32,128]{2,1,0:T(8,128)(2,1)S(1)}, bf16[1,32,128]{2,1,0:T(8,128)(2,1)S(1)}, u32[]{:S(2)}, u32[]{:S(2)}) %collective-permute-start.22) | collective-permute-done | bytes 8224 | tf_op jit(solution)/shard_map/ppermute | solution.py:50
  79.2 5.4 %collective-permute-start.23 = (bf16[2,32,128]{2,1,0:T(8,128)(2,1)S(1)}, bf16[2,32,128]{2,1,0:T(8,128)(2,1)S(1)}, u32[]{:S(2)}, u32[]{:S(2)}) collective-permute-start(bf16[2,32,128]{2,1,0:T(8,128)(2,1)S(1)} %maximum_select_fusion.10), channel_id=1, source_target_pairs={{0,128},{8,136},{16,144},{24,152},{32,160},{40,168},{48,176},{56,1... | collective-permute-start | bytes 49160 | tf_op jit(solution)/shard_map/ppermute | solution.py:50
  101.7 5.1 %collective-permute-start.26 = (bf16[16,32,128]{2,1,0:T(8,128)(2,1)S(1)}, bf16[16,32,128]{2,1,0:T(8,128)(2,1)S(1)}, u32[]{:S(2)}, u32[]{:S(2)}) collective-permute-start(bf16[16,32,128]{2,1,0:T(8,128)(2,1)S(1)} %maximum_select_fusion.4), channel_id=1, source_target_pairs={{0,16},{8,24},{16,0},{24,8},{32,48},{40,56},{48,32},{56,40},{64,80... | collective-permute-start | bytes 393224 | tf_op jit(solution)/shard_map/ppermute | solution.py:50
  131.2 6.6 %collective-permute-start.19 = (f32[128,128]{1,0:T(8,128)S(1)}, f32[128,128]{1,0:T(8,128)S(1)}, u32[]{:S(2)}, u32[]{:S(2)}) collective-permute-start(f32[128,128]{1,0:T(8,128)S(1)} %get-tuple-element.66), channel_id=1, source_target_pairs={{8,0},{16,8},{24,16},{32,24},{40,32},{48,40},{56,48},{64,56},{72,6... | collective-permute-start | bytes 196616 | tf_op jit(solution)/shard_map/ppermute | solution.py:15
  147.9 28.0 %all-to-all-done = bf16[8,2048,128]{2,1,0:T(8,128)(2,1)} async-done(((bf16[8,2048,128]{2,1,0:T(8,128)(2,1)}), bf16[8,2048,128]{2,1,0:T(8,128)(2,1)}, u32[]{:S(2)}, u32[]{:S(2)}) %all-to-all-start) | async-done | bytes 4194336 | tf_op jit(solution)/shard_map/all_to_all | solution.py:56
  175.9 7.3 %reshape_reshape.6 = bf16[512,4096]{1,0:T(8,128)(2,1)} reshape(bf16[8,2048,128]{2,1,0:T(8,128)(2,1)} %all-to-all-done) | data formatting | bytes 8388608 | tf_op jit(solution)/shard_map/reshape;reshape | solution.py:129
  183.2 6.6 %convolution_convert_fusion.1 = bf16[512,4096]{1,0:T(8,128)(2,1)} fusion(bf16[512,4096]{1,0:T(8,128)(2,1)} %reshape_reshape.6, s32[512]{0:T(512)S(1)} %gather_fusion.1), kind=kOutput, calls=%fused_computation.10 | convolution fusion | flops 2149842944 | bytes 8390656 | tf_op jit(solution)/shard_map/dot_general | solution.py:130
  189.8 7.5 %reshape.130 = bf16[16384,128]{1,0:T(8,128)(2,1)} reshape(bf16[512,4096]{1,0:T(8,128)(2,1)} %convolution_convert_fusion.1) | data formatting | bytes 8388608 | tf_op jit(solution)/shard_map/reshape | solution.py:134
  206.8 6.6 %collective-permute-start.29 = (bf16[128,128]{1,0:T(8,128)(2,1)S(1)}, bf16[128,128]{1,0:T(8,128)(2,1)S(1)}, u32[]{:S(2)}, u32[]{:S(2)}) collective-permute-start(bf16[128,128]{1,0:T(8,128)(2,1)S(1)} %get-tuple-element.74), channel_id=1, source_target_pairs={{8,0},{16,8},{24,16},{32,24},{40,32},{48,40},{56,48},{64,56},{72,6... | collective-permute-start | bytes 98312 | tf_op jit(solution)/shard_map/ppermute | solution.py:15
  215.3 7.2 %collective-permute-done.28 = bf16[128,128]{1,0:T(8,128)(2,1)S(1)} collective-permute-done((bf16[128,128]{1,0:T(8,128)(2,1)S(1)}, bf16[128,128]{1,0:T(8,128)(2,1)S(1)}, u32[]{:S(2)}, u32[]{:S(2)}) %collective-permute-start.28) | collective-permute-done | bytes 32800 | tf_op jit(solution)/shard_map/ppermute | solution.py:15
  225.1 12.4 %psum.36 = f32[3,128]{1,0:T(4,128)S(1)} all-reduce(f32[3,128]{1,0:T(4,128)S(1)} %pad_maximum_fusion.4), channel_id=1, replica_groups=mesh['gx'=64,'gy'=8] {'gy'}, use_global_device_ids=true, to_apply=%region_6.7 | all-reduce | flops 384 | bytes 3072 | tf_op jit(solution)/shard_map/psum | solution.py:25
  244.9 5.1 collective-permute-done.33
  265.5 5.7 %collective-permute-done.36 = f32[3,128]{1,0:T(4,128)S(1)} collective-permute-done((f32[3,128]{1,0:T(4,128)S(1)}, f32[3,128]{1,0:T(4,128)S(1)}, u32[]{:S(2)}, u32[]{:S(2)}) %collective-permute-start.36) | collective-permute-done | bytes 1568 | tf_op jit(solution)/shard_map/ppermute | solution.py:33
  274.0 11.4 %collective-permute-done.37 = f32[3,128]{1,0:T(4,128)S(1)} collective-permute-done((f32[3,128]{1,0:T(4,128)S(1)}, f32[3,128]{1,0:T(4,128)S(1)}, u32[]{:S(2)}, u32[]{:S(2)}) %collective-permute-start.37) | collective-permute-done | bytes 1568 | tf_op jit(solution)/shard_map/ppermute | solution.py:33
  289.7 11.9 %collective-permute-done.42 = bf16[1,32,128]{2,1,0:T(8,128)(2,1)S(1)} collective-permute-done((bf16[1,32,128]{2,1,0:T(8,128)(2,1)S(1)}, bf16[1,32,128]{2,1,0:T(8,128)(2,1)S(1)}, u32[]{:S(2)}, u32[]{:S(2)}) %collective-permute-start.42) | collective-permute-done | bytes 8224 | tf_op jit(solution)/shard_map/ppermute | solution.py:50
  304.8 6.4 %collective-permute-done.43 = bf16[2,32,128]{2,1,0:T(8,128)(2,1)S(1)} collective-permute-done((bf16[2,32,128]{2,1,0:T(8,128)(2,1)S(1)}, bf16[2,32,128]{2,1,0:T(8,128)(2,1)S(1)}, u32[]{:S(2)}, u32[]{:S(2)}) %collective-permute-start.43) | collective-permute-done | bytes 16416 | tf_op jit(solution)/shard_map/ppermute | solution.py:50
  326.0 6.4 %collective-permute-done.46 = bf16[16,32,128]{2,1,0:T(8,128)(2,1)S(1)} collective-permute-done((bf16[16,32,128]{2,1,0:T(8,128)(2,1)S(1)}, bf16[16,32,128]{2,1,0:T(8,128)(2,1)S(1)}, u32[]{:S(2)}, u32[]{:S(2)}) %collective-permute-start.46) | collective-permute-done | bytes 131104 | tf_op jit(solution)/shard_map/ppermute | solution.py:50
  334.6 6.2 %collective-permute-done.47 = bf16[32,32,128]{2,1,0:T(8,128)(2,1)S(1)} collective-permute-done((bf16[32,32,128]{2,1,0:T(8,128)(2,1)S(1)}, bf16[32,32,128]{2,1,0:T(8,128)(2,1)S(1)}, u32[]{:S(2)}, u32[]{:S(2)}) %collective-permute-start.47) | collective-permute-done | bytes 262176 | tf_op jit(solution)/shard_map/ppermute | solution.py:50
  359.6 5.2 %collective-permute-done.38 = f32[128,128]{1,0:T(8,128)S(1)} collective-permute-done((f32[128,128]{1,0:T(8,128)S(1)}, f32[128,128]{1,0:T(8,128)S(1)}, u32[]{:S(2)}, u32[]{:S(2)}) %collective-permute-start.38) | collective-permute-done | bytes 65568 | tf_op jit(solution)/shard_map/ppermute | solution.py:15
  365.2 33.0 %all-to-all-done.1 = bf16[8,2048,128]{2,1,0:T(8,128)(2,1)} async-done(((bf16[8,2048,128]{2,1,0:T(8,128)(2,1)}), bf16[8,2048,128]{2,1,0:T(8,128)(2,1)}, u32[]{:S(2)}, u32[]{:S(2)}) %all-to-all-start.1) | async-done | bytes 4194336 | tf_op jit(solution)/shard_map/all_to_all | solution.py:56
  398.2 7.3 %reshape_reshape.7 = bf16[512,4096]{1,0:T(8,128)(2,1)} reshape(bf16[8,2048,128]{2,1,0:T(8,128)(2,1)} %all-to-all-done.1) | data formatting | bytes 8388608 | tf_op jit(solution)/shard_map/reshape;reshape | solution.py:129
  405.5 6.6 %convolution_convert_fusion = bf16[512,4096]{1,0:T(8,128)(2,1)} fusion(bf16[512,4096]{1,0:T(8,128)(2,1)} %reshape_reshape.7, s32[512]{0:T(512)S(1)} %gather_fusion.1), kind=kOutput, calls=%fused_computation.9 | convolution fusion | flops 2149842944 | bytes 8390656 | tf_op jit(solution)/shard_map/dot_general | solution.py:130
  412.1 7.4 %reshape.132 = bf16[16384,128]{1,0:T(8,128)(2,1)} reshape(bf16[512,4096]{1,0:T(8,128)(2,1)} %convolution_convert_fusion) | data formatting | bytes 8388608 | tf_op jit(solution)/shard_map/reshape | solution.py:134
  434.9 5.2 %collective-permute-done.48 = bf16[128,128]{1,0:T(8,128)(2,1)S(1)} collective-permute-done((bf16[128,128]{1,0:T(8,128)(2,1)S(1)}, bf16[128,128]{1,0:T(8,128)(2,1)S(1)}, u32[]{:S(2)}, u32[]{:S(2)}) %collective-permute-start.48) | collective-permute-done | bytes 32800 | tf_op jit(solution)/shard_map/ppermute | solution.py:15
  442.7 12.4 %psum.37 = f32[6,128]{1,0:T(8,128)S(1)} all-reduce(f32[6,128]{1,0:T(8,128)S(1)} %stack.134), channel_id=1, replica_groups=mesh['gx'=64,'gy'=8] {'gy'}, use_global_device_ids=true, to_apply=%region_18.19 | all-reduce | flops 768 | bytes 6144 | tf_op jit(solution)/shard_map/psum | solution.py:25
  462.5 5.1 %collective-permute-done.53 = f32[6,128]{1,0:T(8,128)S(1)} collective-permute-done((f32[6,128]{1,0:T(8,128)S(1)}, f32[6,128]{1,0:T(8,128)S(1)}, u32[]{:S(2)}, u32[]{:S(2)}) %collective-permute-start.53) | collective-permute-done | bytes 3104 | tf_op jit(solution)/shard_map/ppermute | solution.py:33
  482.9 5.9 %collective-permute-done.56 = f32[6,128]{1,0:T(8,128)S(1)} collective-permute-done((f32[6,128]{1,0:T(8,128)S(1)}, f32[6,128]{1,0:T(8,128)S(1)}, u32[]{:S(2)}, u32[]{:S(2)}) %collective-permute-start.56) | collective-permute-done | bytes 3104 | tf_op jit(solution)/shard_map/ppermute | solution.py:33
  491.3 11.8 %collective-permute-done.57 = f32[6,128]{1,0:T(8,128)S(1)} collective-permute-done((f32[6,128]{1,0:T(8,128)S(1)}, f32[6,128]{1,0:T(8,128)S(1)}, u32[]{:S(2)}, u32[]{:S(2)}) %collective-permute-start.57) | collective-permute-done | bytes 3104 | tf_op jit(solution)/shard_map/ppermute | solution.py:33
  (173 shorter events, 211.7 us)
Async XLA Ops:
  40.4 9.4 %collective-permute-start.16 = (f32[128]{0:T(128)S(1)}, f32[128]{0:T(128)S(1)}, u32[]{:S(2)}, u32[]{:S(2)}) collective-permute-start(f32[128]{0:T(128)S(1)} %add.222), channel_id=1, source_target_pairs={{0,128},{8,136},{16,144},{24,152},{32,160},{40,168},{48,176},{56,1... | collective-permute-start | bytes 1544 | tf_op jit(solution)/shard_map/ppermute | solution.py:33
  49.8 14.2 %collective-permute-start.17 = (f32[128]{0:T(128)S(1)}, f32[128]{0:T(128)S(1)}, u32[]{:S(2)}, u32[]{:S(2)}) collective-permute-start(f32[128]{0:T(128)S(1)} %add.223), channel_id=1, source_target_pairs={{0,256},{8,264},{16,272},{24,280},{32,288},{40,296},{48,304},{56,3... | collective-permute-start | bytes 1544 | tf_op jit(solution)/shard_map/ppermute | solution.py:33
  65.0 14.3 %collective-permute-start.22 = (bf16[1,32,128]{2,1,0:T(8,128)(2,1)S(1)}, bf16[1,32,128]{2,1,0:T(8,128)(2,1)S(1)}, u32[]{:S(2)}, u32[]{:S(2)}) collective-permute-start(bf16[1,32,128]{2,1,0:T(8,128)(2,1)S(1)} %fusion.2), channel_id=1, source_target_pairs={{0,256},{8,264},{16,272},{24,280},{32,288},{40,296},{48,304},{56,3... | collective-permute-start | bytes 24584 | tf_op jit(solution)/shard_map/ppermute | solution.py:50
  79.2 9.5 %collective-permute-start.23 = (bf16[2,32,128]{2,1,0:T(8,128)(2,1)S(1)}, bf16[2,32,128]{2,1,0:T(8,128)(2,1)S(1)}, u32[]{:S(2)}, u32[]{:S(2)}) collective-permute-start(bf16[2,32,128]{2,1,0:T(8,128)(2,1)S(1)} %maximum_select_fusion.10), channel_id=1, source_target_pairs={{0,128},{8,136},{16,144},{24,152},{32,160},{40,168},{48,176},{56,1... | collective-permute-start | bytes 49160 | tf_op jit(solution)/shard_map/ppermute | solution.py:50
  101.7 8.4 %collective-permute-start.26 = (bf16[16,32,128]{2,1,0:T(8,128)(2,1)S(1)}, bf16[16,32,128]{2,1,0:T(8,128)(2,1)S(1)}, u32[]{:S(2)}, u32[]{:S(2)}) collective-permute-start(bf16[16,32,128]{2,1,0:T(8,128)(2,1)S(1)} %maximum_select_fusion.4), channel_id=1, source_target_pairs={{0,16},{8,24},{16,0},{24,8},{32,48},{40,56},{48,32},{56,40},{64,80... | collective-permute-start | bytes 393224 | tf_op jit(solution)/shard_map/ppermute | solution.py:50
  110.0 8.3 %collective-permute-start.27 = (bf16[32,32,128]{2,1,0:T(8,128)(2,1)S(1)}, bf16[32,32,128]{2,1,0:T(8,128)(2,1)S(1)}, u32[]{:S(2)}, u32[]{:S(2)}) collective-permute-start(bf16[32,32,128]{2,1,0:T(8,128)(2,1)S(1)} %maximum_select_fusion.2), channel_id=1, source_target_pairs={{0,8},{8,0},{16,24},{24,16},{32,40},{40,32},{48,56},{56,48},{64,72... | collective-permute-start | bytes 786440 | tf_op jit(solution)/shard_map/ppermute | solution.py:50
  121.0 54.9 %all-to-all-start = ((bf16[8,2048,128]{2,1,0:T(8,128)(2,1)}), bf16[8,2048,128]{2,1,0:T(8,128)(2,1)}, u32[]{:S(2)}, u32[]{:S(2)}) async-start(bf16[8,2048,128]{2,1,0:T(8,128)(2,1)} %stack.107), calls=%async_computation | async-start | bytes 8388608 | tf_op jit(solution)/shard_map/all_to_all | solution.py:56
  126.8 16.4 %collective-permute-start.21 = (f32[128,128]{1,0:T(8,128)S(1)}, f32[128,128]{1,0:T(8,128)S(1)}, u32[]{:S(2)}, u32[]{:S(2)}) collective-permute-start(f32[128,128]{1,0:T(8,128)S(1)} %get-tuple-element.67), channel_id=1, source_target_pairs={{1,0},{2,1},{3,2},{4,3},{5,4},{6,5},{7,6},{9,8},{10,9},{11,10},{12... | collective-permute-start | bytes 196616 | tf_op jit(solution)/shard_map/ppermute | solution.py:15
  128.1 15.1 %collective-permute-start.20 = (f32[128,128]{1,0:T(8,128)S(1)}, f32[128,128]{1,0:T(8,128)S(1)}, u32[]{:S(2)}, u32[]{:S(2)}) collective-permute-start(f32[128,128]{1,0:T(8,128)S(1)} %get-tuple-element.65), channel_id=1, source_target_pairs={{0,1},{1,2},{2,3},{3,4},{4,5},{5,6},{6,7},{8,9},{9,10},{10,11},{11... | collective-permute-start | bytes 196616 | tf_op jit(solution)/shard_map/ppermute | solution.py:15
  131.2 12.1 %collective-permute-start.19 = (f32[128,128]{1,0:T(8,128)S(1)}, f32[128,128]{1,0:T(8,128)S(1)}, u32[]{:S(2)}, u32[]{:S(2)}) collective-permute-start(f32[128,128]{1,0:T(8,128)S(1)} %get-tuple-element.66), channel_id=1, source_target_pairs={{8,0},{16,8},{24,16},{32,24},{40,32},{48,40},{56,48},{64,56},{72,6... | collective-permute-start | bytes 196616 | tf_op jit(solution)/shard_map/ppermute | solution.py:15
  137.7 9.8 %collective-permute-start.18 = (f32[128,128]{1,0:T(8,128)S(1)}, f32[128,128]{1,0:T(8,128)S(1)}, u32[]{:S(2)}, u32[]{:S(2)}) collective-permute-start(f32[128,128]{1,0:T(8,128)S(1)} %get-tuple-element.64), channel_id=1, source_target_pairs={{0,8},{8,16},{16,24},{24,32},{32,40},{40,48},{48,56},{56,64},{64,7... | collective-permute-start | bytes 196616 | tf_op jit(solution)/shard_map/ppermute | solution.py:15
  202.4 12.9 %collective-permute-start.31 = (bf16[128,128]{1,0:T(8,128)(2,1)S(1)}, bf16[128,128]{1,0:T(8,128)(2,1)S(1)}, u32[]{:S(2)}, u32[]{:S(2)}) collective-permute-start(bf16[128,128]{1,0:T(8,128)(2,1)S(1)} %get-tuple-element.75), channel_id=1, source_target_pairs={{1,0},{2,1},{3,2},{4,3},{5,4},{6,5},{7,6},{9,8},{10,9},{11,10},{12... | collective-permute-start | bytes 98312 | tf_op jit(solution)/shard_map/ppermute | solution.py:15
  203.7 11.6 %collective-permute-start.30 = (bf16[128,128]{1,0:T(8,128)(2,1)S(1)}, bf16[128,128]{1,0:T(8,128)(2,1)S(1)}, u32[]{:S(2)}, u32[]{:S(2)}) collective-permute-start(bf16[128,128]{1,0:T(8,128)(2,1)S(1)} %get-tuple-element.73), channel_id=1, source_target_pairs={{0,1},{1,2},{2,3},{3,4},{4,5},{5,6},{6,7},{8,9},{9,10},{10,11},{11... | collective-permute-start | bytes 98312 | tf_op jit(solution)/shard_map/ppermute | solution.py:15
  206.8 8.6 %collective-permute-start.29 = (bf16[128,128]{1,0:T(8,128)(2,1)S(1)}, bf16[128,128]{1,0:T(8,128)(2,1)S(1)}, u32[]{:S(2)}, u32[]{:S(2)}) collective-permute-start(bf16[128,128]{1,0:T(8,128)(2,1)S(1)} %get-tuple-element.74), channel_id=1, source_target_pairs={{8,0},{16,8},{24,16},{32,24},{40,32},{48,40},{56,48},{64,56},{72,6... | collective-permute-start | bytes 98312 | tf_op jit(solution)/shard_map/ppermute | solution.py:15
  213.3 9.1 %collective-permute-start.28 = (bf16[128,128]{1,0:T(8,128)(2,1)S(1)}, bf16[128,128]{1,0:T(8,128)(2,1)S(1)}, u32[]{:S(2)}, u32[]{:S(2)}) collective-permute-start(bf16[128,128]{1,0:T(8,128)(2,1)S(1)} %get-tuple-element.72), channel_id=1, source_target_pairs={{0,8},{8,16},{16,24},{24,32},{32,40},{40,48},{48,56},{56,64},{64,7... | collective-permute-start | bytes 98312 | tf_op jit(solution)/shard_map/ppermute | solution.py:15
  243.0 7.0 %collective-permute-start.33 = (f32[3,128]{1,0:T(4,128)S(1)}, f32[3,128]{1,0:T(4,128)S(1)}, u32[]{:S(2)}, u32[]{:S(2)}) collective-permute-start(f32[3,128]{1,0:T(4,128)S(1)} %add.237), channel_id=1, source_target_pairs={{0,16},{8,24},{16,0},{24,8},{32,48},{40,56},{48,32},{56,40},{64,80... | collective-permute-start | bytes 4616 | tf_op jit(solution)/shard_map/ppermute | solution.py:33
  261.8 9.4 %collective-permute-start.36 = (f32[3,128]{1,0:T(4,128)S(1)}, f32[3,128]{1,0:T(4,128)S(1)}, u32[]{:S(2)}, u32[]{:S(2)}) collective-permute-start(f32[3,128]{1,0:T(4,128)S(1)} %add.240), channel_id=1, source_target_pairs={{0,128},{8,136},{16,144},{24,152},{32,160},{40,168},{48,176},{56,1... | collective-permute-start | bytes 4616 | tf_op jit(solution)/shard_map/ppermute | solution.py:33
  271.2 14.2 %collective-permute-start.37 = (f32[3,128]{1,0:T(4,128)S(1)}, f32[3,128]{1,0:T(4,128)S(1)}, u32[]{:S(2)}, u32[]{:S(2)}) collective-permute-start(f32[3,128]{1,0:T(4,128)S(1)} %add.241), channel_id=1, source_target_pairs={{0,256},{8,264},{16,272},{24,280},{32,288},{40,296},{48,304},{56,3... | collective-permute-start | bytes 4616 | tf_op jit(solution)/shard_map/ppermute | solution.py:33
  286.9 14.6 %collective-permute-start.42 = (bf16[1,32,128]{2,1,0:T(8,128)(2,1)S(1)}, bf16[1,32,128]{2,1,0:T(8,128)(2,1)S(1)}, u32[]{:S(2)}, u32[]{:S(2)}) collective-permute-start(bf16[1,32,128]{2,1,0:T(8,128)(2,1)S(1)} %fusion.3), channel_id=1, source_target_pairs={{0,256},{8,264},{16,272},{24,280},{32,288},{40,296},{48,304},{56,3... | collective-permute-start | bytes 24584 | tf_op jit(solution)/shard_map/ppermute | solution.py:50
  301.5 9.6 %collective-permute-start.43 = (bf16[2,32,128]{2,1,0:T(8,128)(2,1)S(1)}, bf16[2,32,128]{2,1,0:T(8,128)(2,1)S(1)}, u32[]{:S(2)}, u32[]{:S(2)}) collective-permute-start(bf16[2,32,128]{2,1,0:T(8,128)(2,1)S(1)} %maximum_select_fusion.11), channel_id=1, source_target_pairs={{0,128},{8,136},{16,144},{24,152},{32,160},{40,168},{48,176},{56,1... | collective-permute-start | bytes 49160 | tf_op jit(solution)/shard_map/ppermute | solution.py:50
  324.1 8.4 %collective-permute-start.46 = (bf16[16,32,128]{2,1,0:T(8,128)(2,1)S(1)}, bf16[16,32,128]{2,1,0:T(8,128)(2,1)S(1)}, u32[]{:S(2)}, u32[]{:S(2)}) collective-permute-start(bf16[16,32,128]{2,1,0:T(8,128)(2,1)S(1)} %maximum_select_fusion.5), channel_id=1, source_target_pairs={{0,16},{8,24},{16,0},{24,8},{32,48},{40,56},{48,32},{56,40},{64,80... | collective-permute-start | bytes 393224 | tf_op jit(solution)/shard_map/ppermute | solution.py:50
  332.5 8.3 %collective-permute-start.47 = (bf16[32,32,128]{2,1,0:T(8,128)(2,1)S(1)}, bf16[32,32,128]{2,1,0:T(8,128)(2,1)S(1)}, u32[]{:S(2)}, u32[]{:S(2)}) collective-permute-start(bf16[32,32,128]{2,1,0:T(8,128)(2,1)S(1)} %maximum_select_fusion.3), channel_id=1, source_target_pairs={{0,8},{8,0},{16,24},{24,16},{32,40},{40,32},{48,56},{56,48},{64,72... | collective-permute-start | bytes 786440 | tf_op jit(solution)/shard_map/ppermute | solution.py:50
  343.4 54.8 %all-to-all-start.1 = ((bf16[8,2048,128]{2,1,0:T(8,128)(2,1)}), bf16[8,2048,128]{2,1,0:T(8,128)(2,1)}, u32[]{:S(2)}, u32[]{:S(2)}) async-start(bf16[8,2048,128]{2,1,0:T(8,128)(2,1)} %stack.123), calls=%async_computation.1 | async-start | bytes 8388608 | tf_op jit(solution)/shard_map/all_to_all | solution.py:56
  349.0 10.2 %collective-permute-start.41 = (f32[128,128]{1,0:T(8,128)S(1)}, f32[128,128]{1,0:T(8,128)S(1)}, u32[]{:S(2)}, u32[]{:S(2)}) collective-permute-start(f32[128,128]{1,0:T(8,128)S(1)} %get-tuple-element.63), channel_id=1, source_target_pairs={{1,0},{2,1},{3,2},{4,3},{5,4},{6,5},{7,6},{9,8},{10,9},{11,10},{12... | collective-permute-start | bytes 196616 | tf_op jit(solution)/shard_map/ppermute | solution.py:15
  350.3 8.9 %collective-permute-start.40 = (f32[128,128]{1,0:T(8,128)S(1)}, f32[128,128]{1,0:T(8,128)S(1)}, u32[]{:S(2)}, u32[]{:S(2)}) collective-permute-start(f32[128,128]{1,0:T(8,128)S(1)} %get-tuple-element.61), channel_id=1, source_target_pairs={{0,1},{1,2},{2,3},{3,4},{4,5},{5,6},{6,7},{8,9},{9,10},{10,11},{11... | collective-permute-start | bytes 196616 | tf_op jit(solution)/shard_map/ppermute | solution.py:15
  355.3 9.5 %collective-permute-start.38 = (f32[128,128]{1,0:T(8,128)S(1)}, f32[128,128]{1,0:T(8,128)S(1)}, u32[]{:S(2)}, u32[]{:S(2)}) collective-permute-start(f32[128,128]{1,0:T(8,128)S(1)} %get-tuple-element.60), channel_id=1, source_target_pairs={{0,8},{8,16},{16,24},{24,32},{32,40},{40,48},{48,56},{56,64},{64,7... | collective-permute-start | bytes 196616 | tf_op jit(solution)/shard_map/ppermute | solution.py:15
  424.6 10.2 %collective-permute-start.51 = (bf16[128,128]{1,0:T(8,128)(2,1)S(1)}, bf16[128,128]{1,0:T(8,128)(2,1)S(1)}, u32[]{:S(2)}, u32[]{:S(2)}) collective-permute-start(bf16[128,128]{1,0:T(8,128)(2,1)S(1)} %get-tuple-element.71), channel_id=1, source_target_pairs={{1,0},{2,1},{3,2},{4,3},{5,4},{6,5},{7,6},{9,8},{10,9},{11,10},{12... | collective-permute-start | bytes 98312 | tf_op jit(solution)/shard_map/ppermute | solution.py:15
  425.9 8.9 %collective-permute-start.50 = (bf16[128,128]{1,0:T(8,128)(2,1)S(1)}, bf16[128,128]{1,0:T(8,128)(2,1)S(1)}, u32[]{:S(2)}, u32[]{:S(2)}) collective-permute-start(bf16[128,128]{1,0:T(8,128)(2,1)S(1)} %get-tuple-element.69), channel_id=1, source_target_pairs={{0,1},{1,2},{2,3},{3,4},{4,5},{5,6},{6,7},{8,9},{9,10},{10,11},{11... | collective-permute-start | bytes 98312 | tf_op jit(solution)/shard_map/ppermute | solution.py:15
  430.9 9.1 %collective-permute-start.48 = (bf16[128,128]{1,0:T(8,128)(2,1)S(1)}, bf16[128,128]{1,0:T(8,128)(2,1)S(1)}, u32[]{:S(2)}, u32[]{:S(2)}) collective-permute-start(bf16[128,128]{1,0:T(8,128)(2,1)S(1)} %get-tuple-element.68), channel_id=1, source_target_pairs={{0,8},{8,16},{16,24},{24,32},{32,40},{40,48},{48,56},{56,64},{64,7... | collective-permute-start | bytes 98312 | tf_op jit(solution)/shard_map/ppermute | solution.py:15
  460.6 7.0 %collective-permute-start.53 = (f32[6,128]{1,0:T(8,128)S(1)}, f32[6,128]{1,0:T(8,128)S(1)}, u32[]{:S(2)}, u32[]{:S(2)}) collective-permute-start(f32[6,128]{1,0:T(8,128)S(1)} %add.247), channel_id=1, source_target_pairs={{0,16},{8,24},{16,0},{24,8},{32,48},{40,56},{48,32},{56,40},{64,80... | collective-permute-start | bytes 9224 | tf_op jit(solution)/shard_map/ppermute | solution.py:33
  479.5 9.4 %collective-permute-start.56 = (f32[6,128]{1,0:T(8,128)S(1)}, f32[6,128]{1,0:T(8,128)S(1)}, u32[]{:S(2)}, u32[]{:S(2)}) collective-permute-start(f32[6,128]{1,0:T(8,128)S(1)} %add.250), channel_id=1, source_target_pairs={{0,128},{8,136},{16,144},{24,152},{32,160},{40,168},{48,176},{56,1... | collective-permute-start | bytes 9224 | tf_op jit(solution)/shard_map/ppermute | solution.py:33
  488.9 14.2 %collective-permute-start.57 = (f32[6,128]{1,0:T(8,128)S(1)}, f32[6,128]{1,0:T(8,128)S(1)}, u32[]{:S(2)}, u32[]{:S(2)}) collective-permute-start(f32[6,128]{1,0:T(8,128)S(1)} %add.251), channel_id=1, source_target_pairs={{0,256},{8,264},{16,272},{24,280},{32,288},{40,296},{48,304},{56,3... | collective-permute-start | bytes 9224 | tf_op jit(solution)/shard_map/ppermute | solution.py:33
  (25 other events, 422.6 us)
